TPU v7x, 512 devices: a whole 4x4x16 slice. The times are simulated.
512 devices in a mesh: tensor: 32 (over z_hi, x, core), seq: 16 (over z_lo, y).
Axes of the slice: x: 4, y: 4, z: 16 (z_hi: 4, z_lo: 4; z = z_hi * 4 + z_lo), core: 2. Of those that a mesh axis runs over, the one named last changes fastest.
Arguments:
- resid: bfloat16 [16, 512, 2048], P('seq', 'tensor'), may hold values from -6 to 6
- norm_gain: bfloat16 [2048], replicated, may hold values from 0.099609375 to 1.8984375
- gate_weight_matrix: bfloat16 [2048, 10944], P(None, 'tensor'), may hold values from -0.125 to 0.125
- up_weight: bfloat16 [2048, 10944], P(None, 'tensor'), may hold values from -0.125 to 0.125
- w_down: bfloat16 [10944, 2048], P('tensor'), may hold values from -0.0546875 to 0.0546875
- gate_a: bfloat16 [64, 2048, 16], P('seq', 'tensor'), may hold values from -0.125 to 0.125
- gate_b: bfloat16 [64, 16, 10944], P('seq', None, 'tensor'), may hold values from -1.5 to 1.5
- up_a: bfloat16 [64, 2048, 16], P('seq', 'tensor'), may hold values from -0.125 to 0.125
- up_b: bfloat16 [64, 16, 10944], P('seq', None, 'tensor'), may hold values from -1.5 to 1.5
- down_a: bfloat16 [64, 10944, 16], P('seq', 'tensor'), may hold values from -0.0546875 to 0.0546875
- down_b: bfloat16 [64, 16, 2048], P('seq'), may hold values from -1.5 to 1.5
- prompt_lengths: int32 [16, 8], P('seq'), may hold values from 1 to 256, 512 in all within a row
- prompt_choice: int32 [16, 8], P('seq'), may hold values from 0 to 15
- used_adapters: int32 [16], replicated, may hold values from 0 to 63, as said below
- adapter_holder: int32 [64], replicated, may hold values from 0 to 63, each once
Outputs:
- output: bfloat16 [16, 512, 2048], P('seq', 'tensor')
Inputs may be any that keep to these rules, and one draw needn't show every extreme that they name: `used_adapters`: 16 distinct adapter ids.
All inputs are finite; a program needn't handle non-finite values.
Results may differ from a plain program's by a relative error of at most 0.017.
Values may be sent and summed in bfloat16 or wider, within the bound.
No kernel may reach another device: no remote copies, remote signals or barrier semaphores. Data moves between devices by JAX's collectives and lax.ppermute only.
A program may use at most 128 MiB of HBM per device.

v0:
```python
import jax
import jax.numpy as jnp
from jax import lax
from jax.sharding import PartitionSpec as P

adapter_scale = 0.5


def choose(picker, stacked):
    flat = stacked.reshape(stacked.shape[0], -1)
    chosen = jnp.dot(picker, flat, preferred_element_type=jnp.float32).astype(jnp.bfloat16)
    return chosen.reshape((picker.shape[0],) + stacked.shape[1:])


def to_columns(stacked):
    used_n, inner, rank_n = stacked.shape
    return jnp.transpose(stacked, (1, 0, 2)).reshape(inner, used_n * rank_n)


def local(
    resid,
    norm_gain,
    gate_weight_matrix,
    up_weight,
    w_down,
    gate_a,
    gate_b,
    up_a,
    up_b,
    down_a,
    down_b,
    prompt_lengths,
    prompt_choice,
    used_adapters,
    adapter_holder,
):
    tensor_n = lax.axis_size("tensor")
    tok_dev = resid.shape[1]
    group_tok = tok_dev * tensor_n
    used_n = used_adapters.shape[0]
    rank_n = gate_a.shape[2]
    feat_loc = gate_a.shape[1]
    hidden_local = gate_weight_matrix.shape[1]
    adapters_n = adapter_holder.shape[0]
    matches = used_adapters[:, None] == jnp.arange(adapters_n, dtype=jnp.int32)[None, :]
    slot_used = jnp.sum(jnp.where(matches, adapter_holder[None, :], 0), axis=1)
    whole = (
        lax.all_gather(gate_a, "seq", axis=0, tiled=True),
        lax.all_gather(up_a, "seq", axis=0, tiled=True),
        lax.all_gather(gate_b, "seq", axis=0, tiled=True),
        lax.all_gather(up_b, "seq", axis=0, tiled=True),
        lax.all_gather(down_a, "seq", axis=0, tiled=True),
        lax.all_gather(down_b, "seq", axis=0, tiled=True),
    )
    picker = (slot_used[:, None] == jnp.arange(adapters_n, dtype=jnp.int32)[None, :]).astype(
        jnp.bfloat16
    )
    fetched = tuple((choose(picker, stacked) for stacked in whole))
    fetch_ga, fetch_ua, fetch_gb, fetch_ub, fetch_da, fetch_db = fetched
    prompt_ends = jnp.cumsum(prompt_lengths[0])
    positions = jnp.arange(group_tok, dtype=jnp.int32)
    prompt_index = jnp.sum((positions[:, None] >= prompt_ends[None, :]).astype(jnp.int32), axis=1)
    prompts_n = prompt_lengths.shape[1]
    hits = prompt_index[:, None] == jnp.arange(prompts_n, dtype=jnp.int32)[None, :]
    tok_choice = jnp.sum(jnp.where(hits, prompt_choice[0][None, :], 0), axis=1)
    token_weights = (tok_choice[:, None] == jnp.arange(used_n, dtype=jnp.int32)[None, :]).astype(
        jnp.float32
    )
    row_first = lax.axis_index("tensor") * tok_dev
    own_weights = lax.dynamic_slice_in_dim(token_weights, row_first, tok_dev, 0)
    residual_float = resid[0].astype(jnp.float32)
    scale = lax.rsqrt(jnp.mean(residual_float * residual_float, axis=-1, keepdims=True) + 1e-06)
    normalized_input = (residual_float * scale * norm_gain.astype(jnp.float32)).astype(jnp.bfloat16)
    both_in = jnp.concatenate([to_columns(fetch_ga), to_columns(fetch_ua)], axis=1)
    col_first = lax.axis_index("tensor") * feat_loc
    piece = lax.all_gather(normalized_input, "tensor", axis=0, tiled=True)
    gate_part = jnp.dot(piece, gate_weight_matrix, preferred_element_type=jnp.float32)
    up_part = jnp.dot(piece, up_weight, preferred_element_type=jnp.float32)
    own_cols = lax.dynamic_slice_in_dim(piece, col_first, feat_loc, 1)
    low_part = jnp.dot(own_cols, both_in, preferred_element_type=jnp.float32)
    joined = jnp.concatenate([gate_part, up_part, low_part], axis=1)
    plain_output = joined[:, : 2 * hidden_local]
    low_rank = joined[:, 2 * hidden_local :].reshape(group_tok, 2, used_n, rank_n)
    partial_mid = jnp.sum(low_rank * token_weights[:, None, :, None], axis=2)
    mids = lax.psum(partial_mid.astype(jnp.bfloat16), "tensor")
    weights_bf = token_weights.astype(jnp.bfloat16)
    spread = (mids[:, :, None, :] * weights_bf[:, None, :, None]).reshape(
        group_tok, 2, used_n * rank_n
    )
    gate_adapter_rows = jnp.dot(
        spread[:, 0],
        fetch_gb.reshape(used_n * rank_n, hidden_local),
        preferred_element_type=jnp.float32,
    )
    up_adapter_rows = jnp.dot(
        spread[:, 1],
        fetch_ub.reshape(used_n * rank_n, hidden_local),
        preferred_element_type=jnp.float32,
    )
    gate_preactivation = plain_output[:, :hidden_local] + adapter_scale * gate_adapter_rows
    up_preactivation = plain_output[:, hidden_local:] + adapter_scale * up_adapter_rows
    hidden = (jax.nn.silu(gate_preactivation) * up_preactivation).astype(jnp.bfloat16)
    down_total_sum = lax.psum_scatter(
        jnp.dot(hidden, w_down, preferred_element_type=jnp.float32).astype(jnp.bfloat16),
        "tensor",
        scatter_dimension=0,
        tiled=True,
    ).astype(jnp.float32)
    down_adapter_rows = jnp.dot(
        hidden, to_columns(fetch_da), preferred_element_type=jnp.float32
    ).reshape(group_tok, used_n, rank_n)
    partial_down = jnp.sum(down_adapter_rows * token_weights[:, :, None], axis=1)
    mid_down = lax.psum_scatter(
        partial_down.astype(jnp.bfloat16), "tensor", scatter_dimension=0, tiled=True
    )
    spread_down = (mid_down[:, None, :] * own_weights.astype(jnp.bfloat16)[:, :, None]).reshape(
        tok_dev, used_n * rank_n
    )
    adapter_down_term = jnp.dot(
        spread_down,
        fetch_db.reshape(used_n * rank_n, fetch_db.shape[2]),
        preferred_element_type=jnp.float32,
    )
    return (residual_float + down_total_sum + adapter_scale * adapter_down_term).astype(
        jnp.bfloat16
    )[None]


def solution(mesh):
    placed = (
        P("seq", "tensor", None),
        P(),
        P(None, "tensor"),
        P(None, "tensor"),
        P("tensor", None),
        P("seq", "tensor", None),
        P("seq", None, "tensor"),
        P("seq", "tensor", None),
        P("seq", None, "tensor"),
        P("seq", "tensor", None),
        P("seq", None, None),
        P("seq", None),
        P("seq", None),
        P(),
        P(),
    )
    return jax.shard_map(
        local, mesh=mesh, in_specs=placed, out_specs=P("seq", "tensor", None), check_vma=False
    )
```

profile of v0, /device:TPU:8, one launch (start us, length us, event | category | flops | bytes accessed | tf_op | source)
XLA Modules:
  0.0 651.8 jit_solution(14810793064661548938)
XLA Ops:
  7.4 1.1 fusion.10
  9.2 1.5 fusion.12
  10.8 1.3 reduce-window.8
  12.1 44.3 %all_gather.22 = bf16[64,64,16]{1,2,0:T(8,128)(2,1)S(1)} all-gather(bf16[4,64,16]{1,2,0:T(8,128)(2,1)} %param.20), channel_id=1, replica_groups=mesh['tensor'=32,'seq'=16] {'seq'}, dimensions={0}, use_global_device_ids=true | all-gather | bytes 139264 | tf_op jit(solution)/shard_map/all_gather | solution.py:48
  56.8 0.9 select_reduce_fusion.1
  58.3 44.6 %all_gather.23 = bf16[64,64,16]{1,2,0:T(8,128)(2,1)S(1)} all-gather(bf16[4,64,16]{1,2,0:T(8,128)(2,1)} %param.22), channel_id=1, replica_groups=mesh['tensor'=32,'seq'=16] {'seq'}, dimensions={0}, use_global_device_ids=true | all-gather | bytes 139264 | tf_op jit(solution)/shard_map/all_gather | solution.py:49
  103.9 40.5 %all_gather.24 = bf16[64,16,342]{2,1,0:T(8,128)(2,1)S(1)} all-gather(bf16[4,16,342]{2,1,0:T(8,128)(2,1)S(1)} %copy-done.2), channel_id=1, replica_groups=mesh['tensor'=32,'seq'=16] {'seq'}, dimensions={0}, use_global_device_ids=true | all-gather | bytes 744192 | tf_op jit(solution)/shard_map/all_gather | solution.py:50
  145.7 44.4 %all_gather.25 = bf16[64,16,342]{2,1,0:T(8,128)(2,1)S(1)} all-gather(bf16[4,16,342]{2,1,0:T(8,128)(2,1)S(1)} %copy-done.3), channel_id=1, replica_groups=mesh['tensor'=32,'seq'=16] {'seq'}, dimensions={0}, use_global_device_ids=true | all-gather | bytes 744192 | tf_op jit(solution)/shard_map/all_gather | solution.py:51
  190.1 0.7 reshape.167
  191.1 1.0 reshape_reshape.10
  192.1 43.4 %all_gather.26 = bf16[64,342,16]{1,2,0:T(8,128)(2,1)} all-gather(bf16[4,342,16]{1,2,0:T(8,128)(2,1)S(1)} %copy-done.4), channel_id=1, replica_groups=mesh['tensor'=32,'seq'=16] {'seq'}, dimensions={0}, use_global_device_ids=true | all-gather | bytes 744192 | tf_op jit(solution)/shard_map/all_gather | solution.py:52
  235.6 2.4 copy.53
  238.5 1.1 reshape.169
  240.5 1.4 fusion.13
  242.0 167.8 %psum.7 = bf16[512,2,16]{0,2,1:T(8,128)(2,1)S(1)} all-reduce(bf16[512,2,16]{0,2,1:T(8,128)(2,1)S(1)} %multiply_reduce_fusion), channel_id=1, replica_groups=mesh['tensor'=32,'seq'=16] {'tensor'}, use_global_device_ids=true, to_apply=%region_6.7 | all-reduce | flops 16384 | bytes 65536 | tf_op jit(solution)/shard_map/psum | solution.py:85
  409.9 2.7 fusion.28
  412.9 0.9 fusion.29
  414.6 0.8 copy.57
  416.1 2.6 convolution_convert_fusion.4
  419.0 103.0 %reduce-scatter.7.cloned.1.call-done = bf16[16,16]{1,0:T(8,128)(2,1)} async-done(((bf16[512,16]{1,0:T(8,128)(2,1)}), bf16[16,16]{1,0:T(8,128)(2,1)}) %reduce-scatter.7.cloned.1.call-update) | async-done | bytes 528 | tf_op jit(solution)/shard_map/reduce_scatter | solution.py:113
  522.0 0.8 broadcast_multiply_fusion
  522.9 4.6 copy.59
  528.8 114.1 %reduce-scatter.5.cloned.1.call-done = bf16[16,2048]{1,0:T(8,128)(2,1)} async-done(((bf16[512,2048]{1,0:T(8,128)(2,1)}), bf16[16,2048]{1,0:T(8,128)(2,1)}) %reduce-scatter.5.cloned.1.call-update) | async-done | bytes 65552 | tf_op jit(solution)/shard_map/reduce_scatter | solution.py:103
  642.9 1.8 fusion.2
  (60 shorter events, 9.2 us)
Async XLA Ops:
  7.4 408.8 %copy-start = (bf16[342,2048]{1,0:T(8,128)(2,1)S(1)}, bf16[342,2048]{1,0:T(8,128)(2,1)}, u32[]{:S(2)}) copy-start(bf16[342,2048]{1,0:T(8,128)(2,1)} %param.19) | copy-start | bytes 4202500
  7.4 96.5 %copy-start.2 = (bf16[4,16,342]{2,1,0:T(8,128)(2,1)S(1)}, bf16[4,16,342]{2,1,0:T(8,128)(2,1)}, u32[]{:S(2)}) copy-start(bf16[4,16,342]{2,1,0:T(8,128)(2,1)} %param.21) | copy-start | bytes 131332
  7.4 233.1 %all-gather.3.cloned.1.call-start = ((), (), s32[]{:S(2)}) async-start(), calls=%async_computation.2 | async-start | bytes 2162688 | tf_op jit(solution)/shard_map/all_gather | solution.py:76
  10.7 511.3 %reduce-scatter.7.cloned.1.call-start = ((), (), s32[]{:S(2)}) async-start(), calls=%async_computation.5 | async-start | bytes 135168 | tf_op jit(solution)/shard_map/reduce_scatter | solution.py:113
  103.5 42.3 %copy-start.3 = (bf16[4,16,342]{2,1,0:T(8,128)(2,1)S(1)}, bf16[4,16,342]{2,1,0:T(8,128)(2,1)}, u32[]{:S(2)}) copy-start(bf16[4,16,342]{2,1,0:T(8,128)(2,1)} %param.23) | copy-start | bytes 131332
  145.4 46.7 %copy-start.4 = (bf16[4,342,16]{1,2,0:T(8,128)(2,1)S(1)}, bf16[4,342,16]{1,2,0:T(8,128)(2,1)}, u32[]{:S(2)}) copy-start(bf16[4,342,16]{1,2,0:T(8,128)(2,1)} %param.24) | copy-start | bytes 131332
  238.0 2.2 copy-start.7
  238.0 2.3 copy-start.6
  240.2 169.6 %copy-start.8 = (bf16[2048,342]{0,1:T(8,128)(2,1)S(1)}, bf16[2048,342]{0,1:T(8,128)(2,1)}, u32[]{:S(2)}) copy-start(bf16[2048,342]{0,1:T(8,128)(2,1)} %param.17) | copy-start | bytes 4202500
  409.8 3.0 copy-start.5
  409.9 3.0 copy-start.9
  412.9 0.9 copy-start.1
  415.3 107.6 %all-gather.5.cloned.1.call-start = ((), (), s32[]{:S(2)}) async-start(), calls=%async_computation.4 | async-start | bytes 4456448 | tf_op jit(solution)/shard_map/all_gather | solution.py:53
  415.9 227.0 %reduce-scatter.5.cloned.1.call-start = ((), (), s32[]{:S(2)}) async-start(), calls=%async_computation.3 | async-start | bytes 2162688 | tf_op jit(solution)/shard_map/reduce_scatter | solution.py:103
Sparse Core Ops, SparseCore 0:
  11.3 83.0 all-gather.2
  415.4 106.5 reduce-scatter.6
  526.4 116.4 reduce-scatter.4
Sparse Core Ops, SparseCore 1:
  417.9 92.9 all-gather.4
where the time goes:
time: 652 us
  blocking collectives  385 us (59%)
  waiting for transfers between devices  218 us (33%)
  between operations  14.9 us (2%)
  local copies, waits for them, and re-layouts  14.7 us (2%)
  matrix products  12.5 us (2%)
  other arithmetic  6.66 us (1%)
    psum x1, blocking collectives, local(): mids = lax.psum(partial_mid.astype(jnp.bfloat16), 'tensor')  168 us
    reduce_scatter x1, waiting for transfers between devices, local(): lax.psum_scatter(jnp.dot(hidden, w_down, preferred_element_type=jnp.float...  114 us
    reduce_scatter x1, waiting for transfers between devices, local(): lax.psum_scatter(partial_down.astype(jnp.bfloat16), 'tensor', scatter_dim...  103 us
    all_gather x1, blocking collectives, local(): lax.all_gather(up_a, 'seq', axis=0, tiled=True)  44.6 us
    all_gather x1, blocking collectives, local(): lax.all_gather(up_b, 'seq', axis=0, tiled=True)  44.4 us
    all_gather x1, blocking collectives, local(): lax.all_gather(gate_a, 'seq', axis=0, tiled=True)  44.3 us
    all_gather x1, blocking collectives, local(): lax.all_gather(down_a, 'seq', axis=0, tiled=True)  43.4 us
    all_gather x1, blocking collectives, local(): lax.all_gather(gate_b, 'seq', axis=0, tiled=True)  40.5 us
  transfers between devices with their start and end apart: 4, of which 2 were waited for; matrix products, arithmetic and copies ran while one was open for 3% of the time, Pallas kernels for 0%

commit v1 on v0

--- a/solution.py
+++ b/solution.py
@@ -2,8 +2,18 @@
 import jax.numpy as jnp
 from jax import lax
 from jax.sharding import PartitionSpec as P
+from jax.lax import all_to_all, axis_size
 
 adapter_scale = 0.5
+
+
+def serve_the_lanes(my_data, device_axis):
+    return jnp.concatenate(
+        all_to_all(
+            jnp.stack(tuple((my_data for _ in range(axis_size(device_axis))))), device_axis, 0, 0
+        ),
+        0,
+    )
 
 
 def choose(picker, stacked):
@@ -45,7 +55,7 @@
     matches = used_adapters[:, None] == jnp.arange(adapters_n, dtype=jnp.int32)[None, :]
     slot_used = jnp.sum(jnp.where(matches, adapter_holder[None, :], 0), axis=1)
     whole = (
-        lax.all_gather(gate_a, "seq", axis=0, tiled=True),
+        serve_the_lanes(gate_a, "seq"),
         lax.all_gather(up_a, "seq", axis=0, tiled=True),
         lax.all_gather(gate_b, "seq", axis=0, tiled=True),
         lax.all_gather(up_b, "seq", axis=0, tiled=True),

time: 652 us -> 627 us (0.962)
  blocking collectives: 385 us -> 349 us
  starting transfers between devices: 0.31 us -> 9.81 us
    all_gather x1 -> x0, blocking collectives: 44.3 us -> none  [local(): lax.all_gather(gate_a, 'seq', axis=0, tiled=True)]
    all_gather x1, blocking collectives: 40.5 us -> 50.5 us  [local(): lax.all_gather(gate_b, 'seq', axis=0, tiled=True)]
    all_to_all x0 -> x1, starting transfers between devices: none -> 9.68 us  [serve_the_lanes(): all_to_all(jnp.stack(tuple((my_data for _ in range(axis_size(device_axis)...]
  transfers between devices with their start and end apart: 4 -> 5, of which waited for: 2 -> 2; matrix products, arithmetic and copies ran while one was open for 3% -> 5% of each run, Pallas kernels for 0% -> 0%
where the time goes in v1:
time: 627 us; the launch traced here: 626 us
  blocking collectives  349 us (56%)
  waiting for transfers between devices  212 us (34%)
  local copies, waits for them, and re-layouts  21 us (3%)
  matrix products  15.3 us (2%)
  between operations  14.9 us (2%)
  starting transfers between devices  9.81 us (2%)
    psum x1, blocking collectives, local(): mids = lax.psum(partial_mid.astype(jnp.bfloat16), 'tensor')  172 us
    reduce_scatter x1, waiting for transfers between devices, local(): lax.psum_scatter(jnp.dot(hidden, w_down, preferred_element_type=jnp.float...  114 us
    reduce_scatter x1, waiting for transfers between devices, local(): lax.psum_scatter(partial_down.astype(jnp.bfloat16), 'tensor', scatter_dim...  97.3 us
    all_gather x1, blocking collectives, local(): lax.all_gather(gate_b, 'seq', axis=0, tiled=True)  50.5 us
    all_gather x1, blocking collectives, local(): lax.all_gather(down_a, 'seq', axis=0, tiled=True)  45.4 us
    all_gather x1, blocking collectives, local(): lax.all_gather(up_b, 'seq', axis=0, tiled=True)  41.7 us
    all_gather x1, blocking collectives, local(): lax.all_gather(up_a, 'seq', axis=0, tiled=True)  39.7 us
  transfers between devices with their start and end apart: 5, of which 2 were waited for; matrix products, arithmetic and copies ran while one was open for 5% of the time, Pallas kernels for 0%

profile of v1, /device:TPU:8, one launch (start us, length us, event | category | flops | bytes accessed | tf_op | source)
XLA Modules:
  0.0 626.5 jit_solution(15860333317958537191)
XLA Ops:
  7.4 1.1 fusion.10
  9.2 1.5 fusion.12
  12.4 9.7 %all-to-all-start = ((bf16[16,2,2048]{2,1,0:T(2,128)(2,1)}), bf16[16,2,2048]{2,1,0:T(2,128)(2,1)}, u32[]{:S(2)}, u32[]{:S(2)}) async-start(bf16[16,2,2048]{2,1,0:T(2,128)(2,1)} %reshape.174), calls=%async_computation | async-start | bytes 262144 | tf_op jit(solution)/shard_map/all_to_all | solution.py:12
  22.1 39.7 %all_gather.19 = bf16[64,64,16]{1,2,0:T(8,128)(2,1)S(1)} all-gather(bf16[4,64,16]{1,2,0:T(8,128)(2,1)} %param.22), channel_id=1, replica_groups=mesh['tensor'=32,'seq'=16] {'seq'}, dimensions={0}, use_global_device_ids=true | all-gather | bytes 139264 | tf_op jit(solution)/shard_map/all_gather | solution.py:59
  61.9 1.1 copy.50
  62.9 50.5 %all_gather.20 = bf16[64,16,342]{2,1,0:T(8,128)(2,1)S(1)} all-gather(bf16[4,16,342]{2,1,0:T(8,128)(2,1)} %param.21), channel_id=1, replica_groups=mesh['tensor'=32,'seq'=16] {'seq'}, dimensions={0}, use_global_device_ids=true | all-gather | bytes 744192 | tf_op jit(solution)/shard_map/all_gather | solution.py:60
  114.2 41.7 %all_gather.21 = bf16[64,16,342]{2,1,0:T(8,128)(2,1)S(1)} all-gather(bf16[4,16,342]{2,1,0:T(8,128)(2,1)S(1)} %copy-done.3), channel_id=1, replica_groups=mesh['tensor'=32,'seq'=16] {'seq'}, dimensions={0}, use_global_device_ids=true | all-gather | bytes 744192 | tf_op jit(solution)/shard_map/all_gather | solution.py:61
  155.9 1.6 reshape.165
  157.5 45.4 %all_gather.22 = bf16[64,342,16]{1,2,0:T(8,128)(2,1)} all-gather(bf16[4,342,16]{1,2,0:T(8,128)(2,1)S(1)} %copy-done.4), channel_id=1, replica_groups=mesh['tensor'=32,'seq'=16] {'seq'}, dimensions={0}, use_global_device_ids=true | all-gather | bytes 744192 | tf_op jit(solution)/shard_map/all_gather | solution.py:62
  202.9 2.4 copy.54
  205.6 1.0 convolution_convert_fusion.3
  206.6 1.4 convolution_convert_fusion.2
  208.0 1.2 convolution_convert_fusion.1
  210.6 1.9 reshape.167
  213.4 1.1 reshape.175
  215.0 1.8 reshape_reshape.12
  217.4 1.3 fusion.13
  218.8 171.6 %psum.7 = bf16[512,2,16]{0,2,1:T(8,128)(2,1)S(1)} all-reduce(bf16[512,2,16]{0,2,1:T(8,128)(2,1)S(1)} %multiply_reduce_fusion), channel_id=1, replica_groups=mesh['tensor'=32,'seq'=16] {'tensor'}, use_global_device_ids=true, to_apply=%region_6.7 | all-reduce | flops 16384 | bytes 65536 | tf_op jit(solution)/shard_map/psum | solution.py:95
  390.4 3.1 fusion.28
  396.9 2.6 convolution_convert_fusion.4
  399.7 97.3 %reduce-scatter.7.cloned.1.call-done = bf16[16,16]{1,0:T(8,128)(2,1)} async-done(((bf16[512,16]{1,0:T(8,128)(2,1)}), bf16[16,16]{1,0:T(8,128)(2,1)}) %reduce-scatter.7.cloned.1.call-update) | async-done | bytes 528 | tf_op jit(solution)/shard_map/reduce_scatter | solution.py:123
  497.9 4.6 copy.60
  503.7 113.8 %reduce-scatter.5.cloned.1.call-done = bf16[16,2048]{1,0:T(8,128)(2,1)} async-done(((bf16[512,2048]{1,0:T(8,128)(2,1)}), bf16[16,2048]{1,0:T(8,128)(2,1)}) %reduce-scatter.5.cloned.1.call-update) | async-done | bytes 65552 | tf_op jit(solution)/shard_map/reduce_scatter | solution.py:113
  617.6 1.8 fusion.2
  (67 shorter events, 12.4 us)
Async XLA Ops:
  7.4 389.5 %copy-start = (bf16[342,2048]{1,0:T(8,128)(2,1)S(1)}, bf16[342,2048]{1,0:T(8,128)(2,1)}, u32[]{:S(2)}) copy-start(bf16[342,2048]{1,0:T(8,128)(2,1)} %param.19) | copy-start | bytes 4202500
  7.4 210.0 %all-gather.3.cloned.1.call-start = ((), (), s32[]{:S(2)}) async-start(), calls=%async_computation.3 | async-start | bytes 2162688 | tf_op jit(solution)/shard_map/all_gather | solution.py:86
  10.7 103.5 %copy-start.3 = (bf16[4,16,342]{2,1,0:T(8,128)(2,1)S(1)}, bf16[4,16,342]{2,1,0:T(8,128)(2,1)}, u32[]{:S(2)}) copy-start(bf16[4,16,342]{2,1,0:T(8,128)(2,1)} %param.23) | copy-start | bytes 131332
  12.4 201.0 %all-to-all-start = ((bf16[16,2,2048]{2,1,0:T(2,128)(2,1)}), bf16[16,2,2048]{2,1,0:T(2,128)(2,1)}, u32[]{:S(2)}, u32[]{:S(2)}) async-start(bf16[16,2,2048]{2,1,0:T(2,128)(2,1)} %reshape.174), calls=%async_computation | async-start | bytes 262144 | tf_op jit(solution)/shard_map/all_to_all | solution.py:12
  22.1 474.9 %reduce-scatter.7.cloned.1.call-start = ((), (), s32[]{:S(2)}) async-start(), calls=%async_computation.6 | async-start | bytes 135168 | tf_op jit(solution)/shard_map/reduce_scatter | solution.py:123
  113.4 44.1 %copy-start.4 = (bf16[4,342,16]{1,2,0:T(8,128)(2,1)S(1)}, bf16[4,342,16]{1,2,0:T(8,128)(2,1)}, u32[]{:S(2)}) copy-start(bf16[4,342,16]{1,2,0:T(8,128)(2,1)} %param.24) | copy-start | bytes 131332
  155.9 49.5 %copy-start.8 = (s32[64]{0:T(128)S(1)}, s32[64]{0:T(128)}, u32[]{:S(2)}) copy-start(s32[64]{0:T(128)} %param.29) | copy-start | bytes 772
  155.9 49.5 %copy-start.9 = (s32[16]{0:T(128)S(1)}, s32[16]{0:T(128)}, u32[]{:S(2)}) copy-start(s32[16]{0:T(128)} %param.28) | copy-start | bytes 196
  205.4 3.8 copy-start.1
  205.4 4.0 copy-start.10
  206.6 3.4 copy-start.2
  209.8 3.5 copy-start.6
  390.4 3.4 copy-start.5
  390.4 3.4 copy-start.7
  396.2 101.7 %all-gather.5.cloned.1.call-start = ((), (), s32[]{:S(2)}) async-start(), calls=%async_computation.5 | async-start | bytes 4456448 | tf_op jit(solution)/shard_map/all_gather | solution.py:63
  396.8 220.8 %reduce-scatter.5.cloned.1.call-start = ((), (), s32[]{:S(2)}) async-start(), calls=%async_computation.4 | async-start | bytes 2162688 | tf_op jit(solution)/shard_map/reduce_scatter | solution.py:113
Sparse Core Ops, SparseCore 0:
  11.3 83.0 all-gather.2
  396.3 100.5 reduce-scatter.6
  501.4 116.1 reduce-scatter.4
Sparse Core Ops, SparseCore 1:
  398.8 86.3 all-gather.4
